TPU v7x, 512 devices: a whole 4x4x16 slice. The times are simulated.
512 devices in a mesh: seq: 128 (over z, x, core), fsdp: 4 (over y).
Axes of the slice: x: 4, y: 4, z: 16, core: 2. Of those that a mesh axis runs over, the one named last changes fastest.
Arguments:
- query_key: bfloat16 [131072, 3072], P(('seq', 'fsdp')), may hold values from -48 to 48
- values: bfloat16 [131072, 3072], P(('seq', 'fsdp')), may hold values from -6 to 6
- cluster_ids: int32 [24, 1024], replicated, may hold values from 0 to 127, as said below
Outputs:
- attended: bfloat16 [131072, 3072], P(('seq', 'fsdp'))
Inputs may be any that keep to these rules, and one draw needn't show every extreme that they name: `cluster_ids`: for every head and cluster at most 10 blocks name that cluster, and for every head some cluster is named by exactly 10 blocks. Among the (head, block) pairs of one group of 6 consecutive heads and one run of 8 blocks starting at a multiple of 8, no cluster is named more than 1 times, and some cluster exactly 1 times; the blocks of one such run name distinct clusters for each head.
All inputs are finite; a program needn't handle non-finite values.
Results may differ from a plain program's by a relative error of at most 0.0027.
Values may be sent and summed in bfloat16 or wider, within the bound.
No kernel may reach another device: no remote copies, remote signals or barrier semaphores. Data moves between devices by JAX's collectives and lax.ppermute only.
A program may use at most 64 MiB of HBM per device.

v0:
```python
import math
import jax
import jax.numpy as jnp
from jax import lax
from jax.sharding import PartitionSpec as P

BLK = 128
masked_score = -1e30


def by_index(source_table, row_index):
    return source_table[jnp.clip(row_index, 0, source_table.shape[0] - 1)]


def softmax_group(key_rows, positions, alive_rows, score_scale):
    scores = jnp.dot(key_rows, key_rows.T, preferred_element_type=jnp.float32) * score_scale
    allowed = alive_rows[None, :] & (positions[None, :] <= positions[:, None])
    scores = jnp.where(allowed, scores, masked_score)
    row_peak = jnp.max(scores, axis=1, keepdims=True)
    weights = jnp.where(allowed, jnp.exp(scores - row_peak), 0.0)
    row_total = jnp.where(alive_rows[:, None], jnp.sum(weights, axis=1, keepdims=True), 1.0)
    return (weights.astype(jnp.bfloat16), row_total)


def shards(query_key, values, cluster_ids):
    seq_count = lax.axis_size("seq")
    group_count = lax.axis_size("fsdp")
    seq_index = lax.axis_index("seq")
    group_index = lax.axis_index("fsdp")
    heads_all = cluster_ids.shape[0]
    group_heads = heads_all // group_count
    head_dim = query_key.shape[1] // heads_all
    tok_rows = query_key.shape[0]
    shard_blocks = group_count * tok_rows // BLK
    all_blocks = cluster_ids.shape[1]
    item_count = group_heads * shard_blocks
    slot_count = max(1, item_count // seq_count)
    capacity = shard_blocks + min(shard_blocks // 4, seq_count - shard_blocks)
    group_rows = capacity * BLK
    send_rows = seq_count * slot_count
    score_scale = 1.0 / math.sqrt(head_dim)
    own_blocks = tok_rows // BLK
    keys_local = lax.all_to_all(query_key, "fsdp", split_axis=1, concat_axis=0, tiled=True)
    value_chunks = values.reshape(tok_rows, group_count, group_heads * head_dim)
    value_chunks, keys_local = lax.optimization_barrier((value_chunks, keys_local))
    by_shift = [lax.dynamic_index_in_dim(value_chunks, group_index, 1, keepdims=False)]
    for shift in range(1, group_count):
        outgoing = lax.dynamic_index_in_dim(
            value_chunks, (group_index + shift) % group_count, 1, keepdims=False
        )
        by_shift.append(
            lax.ppermute(
                outgoing,
                "fsdp",
                [(peer, (peer + shift) % group_count) for peer in range(group_count)],
            )
        )
    source_order = (group_index - jnp.arange(group_count, dtype=jnp.int32)) % group_count
    values_local = jnp.stack(by_shift)[source_order].reshape(
        group_count * tok_rows, group_heads * head_dim
    )

    def into_items(block_data):
        shaped = block_data.reshape(shard_blocks, BLK, group_heads, head_dim)
        return jnp.transpose(shaped, (2, 0, 1, 3)).reshape(item_count, BLK, head_dim)

    key_items = into_items(keys_local)
    value_items = into_items(values_local)
    group_ids = lax.dynamic_slice_in_dim(cluster_ids, group_index * group_heads, group_heads, 0)
    by_source = jnp.transpose(
        group_ids.reshape(group_heads, seq_count, shard_blocks), (1, 0, 2)
    ).reshape(seq_count, item_count)
    own_dest = lax.dynamic_index_in_dim(by_source, seq_index, 0, keepdims=False)
    item_ids = jnp.arange(item_count, dtype=jnp.int32)
    earlier = (own_dest[None, :] == own_dest[:, None]) & (item_ids[None, :] < item_ids[:, None])
    own_pos = own_dest * slot_count + jnp.sum(earlier.astype(jnp.int32), axis=1)
    row_ids = jnp.arange(send_rows, dtype=jnp.int32)
    slot_match = own_pos[None, :] == row_ids[:, None]
    send_pick = jnp.sum(jnp.where(slot_match, item_ids[None, :], 0), axis=1) + item_count * (
        1 - jnp.any(slot_match, axis=1).astype(jnp.int32)
    )
    key_send, group_ids = lax.optimization_barrier((by_index(key_items, send_pick), group_ids))
    arrived_k = lax.all_to_all(key_send, "seq", split_axis=0, concat_axis=0, tiled=True)
    value_send = by_index(value_items, send_pick)
    arrived_k, value_send = lax.optimization_barrier((arrived_k, value_send))
    arrived_v = lax.all_to_all(value_send, "seq", split_axis=0, concat_axis=0, tiled=True)
    by_source = jnp.transpose(
        group_ids.reshape(group_heads, seq_count, shard_blocks), (1, 0, 2)
    ).reshape(seq_count, item_count)
    received_mask = (by_source == seq_index).astype(jnp.int32)
    recv_pos = (
        jnp.arange(seq_count, dtype=jnp.int32)[:, None] * slot_count
        + jnp.cumsum(received_mask, axis=1)
        - received_mask
    )
    recv_by_head = jnp.transpose(
        recv_pos.reshape(seq_count, group_heads, shard_blocks), (1, 0, 2)
    ).reshape(group_heads * all_blocks)
    owned_mask = (group_ids == seq_index).astype(jnp.int32)
    ordinal = jnp.cumsum(owned_mask, axis=1) - owned_mask
    target = jnp.where(
        owned_mask > 0, jnp.arange(group_heads, dtype=jnp.int32)[:, None] * capacity + ordinal, -1
    ).reshape(group_heads * all_blocks)
    slot_ids = jnp.arange(group_heads * capacity, dtype=jnp.int32)
    matches = target[None, :] == slot_ids[:, None]
    present = jnp.any(matches, axis=1)
    source_row = jnp.sum(jnp.where(matches, recv_by_head[None, :], 0), axis=1) + send_rows * (
        1 - present.astype(jnp.int32)
    )
    block_ids = jnp.tile(jnp.arange(all_blocks, dtype=jnp.int32), group_heads)
    block_of = jnp.sum(jnp.where(matches, block_ids[None, :], 0), axis=1)
    key_grouped = by_index(arrived_k, source_row)
    value_grouped = by_index(arrived_v, source_row)
    positions = (block_of[:, None] * BLK + jnp.arange(BLK, dtype=jnp.int32)[None, :]).reshape(
        group_heads, group_rows
    )
    alive_rows = jnp.repeat(present, BLK).reshape(group_heads, group_rows)

    def one_head(operands):
        key_rows, where_at, alive_here = operands
        return softmax_group(key_rows, where_at, alive_here, score_scale)

    weights, totals = lax.map(
        one_head, (key_grouped.reshape(group_heads, group_rows, head_dim), positions, alive_rows)
    )
    value_rows = value_grouped.reshape(group_heads, group_rows, head_dim)
    back_match = source_row[None, :] == row_ids[:, None]
    back_pick = jnp.sum(
        jnp.where(back_match, slot_ids[None, :], 0), axis=1
    ) + group_heads * capacity * (1 - jnp.any(back_match, axis=1).astype(jnp.int32))
    weighted = jnp.einsum("hqk,hkd->hqd", weights, value_rows, preferred_element_type=jnp.float32)
    outputs = (
        (weighted / totals).astype(jnp.bfloat16).reshape(group_heads * capacity, BLK, head_dim)
    )
    returned = lax.all_to_all(
        by_index(outputs, back_pick), "seq", split_axis=0, concat_axis=0, tiled=True
    )
    own_output = by_index(returned, own_pos).reshape(
        group_heads, group_count, own_blocks, BLK, head_dim
    )
    gathered = lax.all_to_all(
        jnp.swapaxes(own_output, 0, 1), "fsdp", split_axis=0, concat_axis=0, tiled=True
    )
    token_major = jnp.transpose(gathered, (2, 3, 0, 1, 4))
    return token_major.reshape(tok_rows, heads_all * head_dim)


def solution(mesh):
    placed = (P(("seq", "fsdp"), None), P(("seq", "fsdp"), None), P())
    return jax.shard_map(
        shards, mesh=mesh, in_specs=placed, out_specs=P(("seq", "fsdp"), None), check_vma=False
    )
```

profile of v0, /device:TPU:70, one launch (start us, length us, event | category | flops | bytes accessed | tf_op | source)
XLA Modules:
  0.0 684.2 jit_solution(3121798839654760957)
XLA Ops:
  0.0 2.6 copy.60
  2.6 4.6 all-to-all-start
  8.2 1.1 copy.64
  9.8 1.6 copy.59
  11.8 16.1 %all-to-all-done = bf16[256,4,768]{0,2,1:T(8,128)(2,1)S(1)} async-done(((bf16[256,4,768]{0,2,1:T(8,128)(2,1)}), bf16[256,4,768]{0,2,1:T(8,128)(2,1)S(1)}, u32[]{:S(2)}, u32[]{:S(2)}) %all-to-all-start) | async-done | bytes 1572896 | tf_op jit(solution)/shard_map/all_to_all | solution.py:43
  29.8 1.1 copy.63
  31.0 3.1 gather_fusion
  34.1 18.9 %all-to-all-start.1 = ((bf16[128,128,128]{2,1,0:T(8,128)(2,1)}), bf16[128,128,128]{2,1,0:T(8,128)(2,1)}, u32[]{:S(2)}, u32[]{:S(2)}) async-start(bf16[128,128,128]{2,1,0:T(8,128)(2,1)} %gather_fusion), calls=%async_computation.1 | async-start | bytes 8388608 | tf_op jit(solution)/shard_map/all_to_all | solution.py:83
  53.3 1.7 reduce-window.6
  56.7 2.5 collective-permute-start
  59.4 4.0 collective-permute-start.1
  63.5 2.5 collective-permute-start.2
  67.9 11.5 %collective-permute-done = bf16[256,768]{1,0:T(8,128)(2,1)S(1)} collective-permute-done((bf16[256,768]{1,0:T(8,128)(2,1)S(1)}, bf16[256,768]{1,0:T(8,128)(2,1)S(1)}, u32[]{:S(2)}, u32[]{:S(2)}) %collective-permute-start) | collective-permute-done | bytes 393248 | tf_op jit(solution)/shard_map/ppermute | solution.py:52
  79.4 2.7 collective-permute-done.2
  82.9 1.2 pad_maximum_fusion
  86.4 1.1 copy.73
  87.5 3.1 gather_fusion.2
  90.7 150.5 %all-to-all-done.1 = bf16[128,128,128]{2,1,0:T(8,128)(2,1)} async-done(((bf16[128,128,128]{2,1,0:T(8,128)(2,1)}), bf16[128,128,128]{2,1,0:T(8,128)(2,1)}, u32[]{:S(2)}, u32[]{:S(2)}) %all-to-all-start.1) | async-done | bytes 4194336 | tf_op jit(solution)/shard_map/all_to_all | solution.py:83
  241.2 8.9 %all-to-all-start.2 = ((bf16[128,128,128]{2,1,0:T(8,128)(2,1)}), bf16[128,128,128]{2,1,0:T(8,128)(2,1)}, u32[]{:S(2)}, u32[]{:S(2)}) async-start(bf16[128,128,128]{2,1,0:T(8,128)(2,1)} %gather_fusion.2), calls=%async_computation.2 | async-start | bytes 8388608 | tf_op jit(solution)/shard_map/all_to_all | solution.py:86
  250.2 3.1 gather_fusion.3
  253.3 46.0 %while.12 = (s32[]{:T(128)}, bf16[6,1280,1280]{1,2,0:T(8,128)(2,1)}, f32[6,1280,1]{1,0,2:T(8,128)S(1)}, pred[6,1280]{1,0:T(8,128)(4,1)S(1)}, s32[6,1280]{1,0:T(8...) while((s32[]{:T(128)}, bf16[6,1280,1280]{1,2,0:T(8,128)(2,1)}, ...), condition=%wide.region_12.13_spmd, body=%wide.region_9.12_spmd.sunk | while | flops 444005120 | bytes 23367272 | solution.py:123
  253.4 1.7 fusion.30
  255.1 3.4 fusion.31
  258.5 2.3 fusion.32
  261.0 1.7 fusion.30
  262.7 3.4 fusion.31
  266.1 2.3 fusion.32
  268.7 1.7 fusion.30
  270.4 3.4 fusion.31
  273.9 2.3 fusion.32
  276.4 1.7 fusion.30
  278.1 3.4 fusion.31
  281.5 2.3 fusion.32
  284.1 1.7 fusion.30
  285.8 3.4 fusion.31
  289.2 2.3 fusion.32
  291.7 1.7 fusion.30
  293.5 3.4 fusion.31
  296.8 2.3 fusion.32
  299.3 138.9 %all-to-all-done.2 = bf16[128,128,128]{2,1,0:T(8,128)(2,1)} async-done(((bf16[128,128,128]{2,1,0:T(8,128)(2,1)}), bf16[128,128,128]{2,1,0:T(8,128)(2,1)}, u32[]{:S(2)}, u32[]{:S(2)}) %all-to-all-start.2) | async-done | bytes 4194336 | tf_op jit(solution)/shard_map/all_to_all | solution.py:86
  438.2 4.4 gather_fusion.4
  442.6 11.0 %divide_convert_fusion = bf16[6,1280,128]{2,1,0:T(8,128)(2,1)S(1)} fusion(bf16[6,1280,1280]{1,2,0:T(8,128)(2,1)} %get-tuple-element.49, bf16[6,1280,128]{2,1,0:T(8,128)(2,1)} %bitcast.118, f32[6,1280]{1,0:T(8,128)S(1)} %bitcast.134), kind=kOutput, calls=%fused_computation.22 | convolution fusion | flops 2518548480 | bytes 23623680 | tf_op jit(solution)/shard_map/hqk,hkd->hqd/dot_general | solution.py:131
  453.6 3.1 gather_fusion.5
  456.6 8.9 %all-to-all-start.3 = ((bf16[128,128,128]{2,1,0:T(8,128)(2,1)}), bf16[128,128,128]{2,1,0:T(8,128)(2,1)}, u32[]{:S(2)}, u32[]{:S(2)}) async-start(bf16[128,128,128]{2,1,0:T(8,128)(2,1)} %gather_fusion.5), calls=%async_computation.3 | async-start | bytes 8388608 | tf_op jit(solution)/shard_map/all_to_all | solution.py:135
  465.6 188.1 %all-to-all-done.3 = bf16[128,128,128]{2,1,0:T(8,128)(2,1)} async-done(((bf16[128,128,128]{2,1,0:T(8,128)(2,1)}), bf16[128,128,128]{2,1,0:T(8,128)(2,1)}, u32[]{:S(2)}, u32[]{:S(2)}) %all-to-all-start.3) | async-done | bytes 4194336 | tf_op jit(solution)/shard_map/all_to_all | solution.py:135
  653.7 3.0 gather_fusion.6
  656.9 23.6 %all_to_all.39 = bf16[4,6,2,128,128]{4,3,2,1,0:T(8,128)(2,1)S(1)} all-to-all(bf16[4,6,2,128,128]{4,3,2,1,0:T(8,128)(2,1)S(1)} %copy.77), channel_id=1, replica_groups=mesh['seq'=128,'fsdp'=4] {'fsdp'}, dimensions={0} | all-to-all | bytes 3145728 | tf_op jit(solution)/shard_map/all_to_all | solution.py:141
  681.6 2.6 reshape.391
  (97 shorter events, 13.2 us)
Async XLA Ops:
  0.0 7.2 %copy-start = (s32[24,1024]{1,0:T(8,128)S(1)}, s32[24,1024]{1,0:T(8,128)}, u32[]{:S(2)}) copy-start(s32[24,1024]{1,0:T(8,128)} %param.7) | copy-start | bytes 294916
  2.6 7.2 %copy-start.3 = (bf16[256,3072]{1,0:T(8,128)(2,1)S(1)}, bf16[256,3072]{1,0:T(8,128)(2,1)}, u32[]{:S(2)}) copy-start(bf16[256,3072]{1,0:T(8,128)(2,1)} %param.6) | copy-start | bytes 4718596
  2.6 25.3 %all-to-all-start = ((bf16[256,4,768]{0,2,1:T(8,128)(2,1)}), bf16[256,4,768]{0,2,1:T(8,128)(2,1)S(1)}, u32[]{:S(2)}, u32[]{:S(2)}) async-start(bf16[256,4,768]{0,2,1:T(8,128)(2,1)} %bitcast.4), calls=%async_computation | async-start | bytes 3145728 | tf_op jit(solution)/shard_map/all_to_all | solution.py:43
  34.1 207.1 %all-to-all-start.1 = ((bf16[128,128,128]{2,1,0:T(8,128)(2,1)}), bf16[128,128,128]{2,1,0:T(8,128)(2,1)}, u32[]{:S(2)}, u32[]{:S(2)}) async-start(bf16[128,128,128]{2,1,0:T(8,128)(2,1)} %gather_fusion), calls=%async_computation.1 | async-start | bytes 8388608 | tf_op jit(solution)/shard_map/all_to_all | solution.py:83
  53.0 3.4 copy-start.2
  56.7 22.7 %collective-permute-start = (bf16[256,768]{1,0:T(8,128)(2,1)S(1)}, bf16[256,768]{1,0:T(8,128)(2,1)S(1)}, u32[]{:S(2)}, u32[]{:S(2)}) collective-permute-start(bf16[256,768]{1,0:T(8,128)(2,1)S(1)} %bitcast.124), channel_id=1, source_target_pairs={{0,1},{1,2},{2,3},{3,0},{4,5},{5,6},{6,7},{7,4},{8,9},{9,10},{10,1... | collective-permute-start | bytes 1179656 | tf_op jit(solution)/shard_map/ppermute | solution.py:52
  59.4 20.0 %collective-permute-start.1 = (bf16[256,768]{1,0:T(8,128)(2,1)S(1)}, bf16[256,768]{1,0:T(8,128)(2,1)S(1)}, u32[]{:S(2)}, u32[]{:S(2)}) collective-permute-start(bf16[256,768]{1,0:T(8,128)(2,1)S(1)} %bitcast.125), channel_id=1, source_target_pairs={{0,2},{1,3},{2,0},{3,1},{4,6},{5,7},{6,4},{7,5},{8,10},{9,11},{10,... | collective-permute-start | bytes 1179656 | tf_op jit(solution)/shard_map/ppermute | solution.py:52
  63.5 18.6 %collective-permute-start.2 = (bf16[256,768]{1,0:T(8,128)(2,1)S(1)}, bf16[256,768]{1,0:T(8,128)(2,1)S(1)}, u32[]{:S(2)}, u32[]{:S(2)}) collective-permute-start(bf16[256,768]{1,0:T(8,128)(2,1)S(1)} %bitcast.126), channel_id=1, source_target_pairs={{0,3},{1,0},{2,1},{3,2},{4,7},{5,4},{6,5},{7,6},{8,11},{9,8},{10,9... | collective-permute-start | bytes 1179656 | tf_op jit(solution)/shard_map/ppermute | solution.py:52
  82.1 0.7 copy-start.4
  241.2 197.1 %all-to-all-start.2 = ((bf16[128,128,128]{2,1,0:T(8,128)(2,1)}), bf16[128,128,128]{2,1,0:T(8,128)(2,1)}, u32[]{:S(2)}, u32[]{:S(2)}) async-start(bf16[128,128,128]{2,1,0:T(8,128)(2,1)} %gather_fusion.2), calls=%async_computation.2 | async-start | bytes 8388608 | tf_op jit(solution)/shard_map/all_to_all | solution.py:86
  456.6 197.1 %all-to-all-start.3 = ((bf16[128,128,128]{2,1,0:T(8,128)(2,1)}), bf16[128,128,128]{2,1,0:T(8,128)(2,1)}, u32[]{:S(2)}, u32[]{:S(2)}) async-start(bf16[128,128,128]{2,1,0:T(8,128)(2,1)} %gather_fusion.5), calls=%async_computation.3 | async-start | bytes 8388608 | tf_op jit(solution)/shard_map/all_to_all | solution.py:135
  680.5 3.7 copy-start.1
where the time goes:
time: 685 us; the launch traced here: 684 us
  waiting for transfers between devices  508 us (74%)
  starting transfers between devices  50.4 us (7%)
  local copies, waits for them, and re-layouts  40.9 us (6%)
  other arithmetic  39.3 us (6%)
  blocking collectives  23.6 us (3%)
  matrix products  21.4 us (3%)
    all_to_all x1, waiting for transfers between devices, shards(): lax.all_to_all(by_index(outputs, back_pick), 'seq', split_axis=0, concat_...  188 us
    all_to_all x1, waiting for transfers between devices, shards(): lax.all_to_all(key_send, 'seq', split_axis=0, concat_axis=0, tiled=True)  151 us
    all_to_all x1, waiting for transfers between devices, shards(): lax.all_to_all(value_send, 'seq', split_axis=0, concat_axis=0, tiled=True)  139 us
    all_to_all x1, blocking collectives, shards(): lax.all_to_all(jnp.swapaxes(own_output, 0, 1), 'fsdp', split_axis=0, conc...  23.6 us
    dynamic_update_slice x12, other arithmetic, shards(): lax.map(one_head, (key_grouped.reshape(group_heads, group_rows, head_dim)...  20.4 us
    gather x6, local copies, waits for them, and re-layouts, by_index(): return source_table[jnp.clip(row_index, 0, source_table.shape[0] - 1)]  19.8 us
    all_to_all x1, starting transfers between devices, shards(): lax.all_to_all(key_send, 'seq', split_axis=0, concat_axis=0, tiled=True)  18.9 us
    all_to_all x1, waiting for transfers between devices, shards(): lax.all_to_all(query_key, 'fsdp', split_axis=1, concat_axis=0, tiled=True)  16.1 us
  transfers between devices with their start and end apart: 7, of which 6 were waited for; matrix products, arithmetic and copies ran while one was open for 10% of the time, Pallas kernels for 0%

commit v1 on v0

--- a/solution.py
+++ b/solution.py
@@ -40,7 +40,13 @@
     send_rows = seq_count * slot_count
     score_scale = 1.0 / math.sqrt(head_dim)
     own_blocks = tok_rows // BLK
-    keys_local = lax.all_to_all(query_key, "fsdp", split_axis=1, concat_axis=0, tiled=True)
+    sections_prepare = lambda tile_in, dim_i, d0: jnp.concatenate(
+        lax.all_to_all(
+            jnp.stack(jnp.split(tile_in, lax.axis_size("fsdp"), dim_i), 0), "fsdp", 0, 0
+        ),
+        axis=d0,
+    )
+    keys_local = sections_prepare(query_key, 1, 0)
     value_chunks = values.reshape(tok_rows, group_count, group_heads * head_dim)
     value_chunks, keys_local = lax.optimization_barrier((value_chunks, keys_local))
     by_shift = [lax.dynamic_index_in_dim(value_chunks, group_index, 1, keepdims=False)]

time: 685 us -> 687 us (level)
  no operation moved by 1% of the time
where the time goes in v1:
time: 687 us; the launch traced here: 686 us
  waiting for transfers between devices  508 us (74%)
  starting transfers between devices  50.4 us (7%)
  local copies, waits for them, and re-layouts  41.2 us (6%)
  other arithmetic  40.6 us (6%)
  blocking collectives  23.6 us (3%)
  matrix products  21.4 us (3%)
    all_to_all x1, waiting for transfers between devices, shards(): lax.all_to_all(by_index(outputs, back_pick), 'seq', split_axis=0, concat_...  188 us
    all_to_all x1, waiting for transfers between devices, shards(): lax.all_to_all(key_send, 'seq', split_axis=0, concat_axis=0, tiled=True)  151 us
    all_to_all x1, waiting for transfers between devices, shards(): lax.all_to_all(value_send, 'seq', split_axis=0, concat_axis=0, tiled=True)  139 us
    all_to_all x1, blocking collectives, shards(): lax.all_to_all(jnp.swapaxes(own_output, 0, 1), 'fsdp', split_axis=0, conc...  23.6 us
    dynamic_update_slice x12, other arithmetic, shards(): lax.map(one_head, (key_grouped.reshape(group_heads, group_rows, head_dim)...  20.4 us
    gather x6, local copies, waits for them, and re-layouts, by_index(): return source_table[jnp.clip(row_index, 0, source_table.shape[0] - 1)]  19.8 us
    all_to_all x1, starting transfers between devices, shards(): lax.all_to_all(key_send, 'seq', split_axis=0, concat_axis=0, tiled=True)  18.9 us
    all_to_all x1, waiting for transfers between devices, shards(): lax.all_to_all(jnp.stack(jnp.split(tile_in, lax.axis_size('fsdp'), dim_i)...  16.1 us
  transfers between devices with their start and end apart: 7, of which 6 were waited for; matrix products, arithmetic and copies ran while one was open for 10% of the time, Pallas kernels for 0%

profile of v1, /device:TPU:70, one launch (start us, length us, event | category | flops | bytes accessed | tf_op | source)
XLA Modules:
  0.0 685.8 jit_solution(1297610700516449343)
XLA Ops:
  0.0 1.5 slice_bitcast_fusion.3
  1.5 1.3 pad_maximum_fusion
  2.8 4.6 all-to-all-start
  10.0 1.6 copy.55
  12.0 16.1 %all-to-all-done = bf16[4,256,768]{2,1,0:T(8,128)(2,1)S(1)} async-done(((bf16[4,256,768]{2,1,0:T(8,128)(2,1)}), bf16[4,256,768]{2,1,0:T(8,128)(2,1)S(1)}, u32[]{:S(2)}, u32[]{:S(2)}) %all-to-all-start) | async-done | bytes 1572896 | tf_op jit(solution)/shard_map/all_to_all | solution.py:44
  28.9 1.6 copy.80
  30.5 2.1 copy.57
  32.6 3.1 gather_fusion
  35.7 18.9 %all-to-all-start.1 = ((bf16[128,128,128]{2,1,0:T(8,128)(2,1)}), bf16[128,128,128]{2,1,0:T(8,128)(2,1)}, u32[]{:S(2)}, u32[]{:S(2)}) async-start(bf16[128,128,128]{2,1,0:T(8,128)(2,1)} %gather_fusion), calls=%async_computation.1 | async-start | bytes 8388608 | tf_op jit(solution)/shard_map/all_to_all | solution.py:89
  55.8 1.7 reduce-window.6
  58.4 2.5 collective-permute-start
  61.0 4.0 collective-permute-start.1
  65.2 2.5 collective-permute-start.2
  69.5 11.5 %collective-permute-done = bf16[256,768]{1,0:T(8,128)(2,1)S(1)} collective-permute-done((bf16[256,768]{1,0:T(8,128)(2,1)S(1)}, bf16[256,768]{1,0:T(8,128)(2,1)S(1)}, u32[]{:S(2)}, u32[]{:S(2)}) %collective-permute-start) | collective-permute-done | bytes 393248 | tf_op jit(solution)/shard_map/ppermute | solution.py:58
  81.1 2.7 collective-permute-done.2
  84.5 1.2 pad_maximum_fusion.1
  89.2 3.1 gather_fusion.2
  92.3 150.5 %all-to-all-done.1 = bf16[128,128,128]{2,1,0:T(8,128)(2,1)} async-done(((bf16[128,128,128]{2,1,0:T(8,128)(2,1)}), bf16[128,128,128]{2,1,0:T(8,128)(2,1)}, u32[]{:S(2)}, u32[]{:S(2)}) %all-to-all-start.1) | async-done | bytes 4194336 | tf_op jit(solution)/shard_map/all_to_all | solution.py:89
  242.8 9.0 %all-to-all-start.2 = ((bf16[128,128,128]{2,1,0:T(8,128)(2,1)}), bf16[128,128,128]{2,1,0:T(8,128)(2,1)}, u32[]{:S(2)}, u32[]{:S(2)}) async-start(bf16[128,128,128]{2,1,0:T(8,128)(2,1)} %gather_fusion.2), calls=%async_computation.2 | async-start | bytes 8388608 | tf_op jit(solution)/shard_map/all_to_all | solution.py:92
  251.8 3.1 gather_fusion.3
  254.9 46.0 %while.12 = (s32[]{:T(128)}, bf16[6,1280,1280]{1,2,0:T(8,128)(2,1)}, f32[6,1280,1]{1,0,2:T(8,128)S(1)}, pred[6,1280]{1,0:T(8,128)(4,1)S(1)}, s32[6,1280]{1,0:T(8...) while((s32[]{:T(128)}, bf16[6,1280,1280]{1,2,0:T(8,128)(2,1)}, ...), condition=%wide.region_12.13_spmd, body=%wide.region_9.12_spmd.sunk | while | flops 444005120 | bytes 23367272 | solution.py:129
  255.0 1.7 fusion.30
  256.8 3.4 fusion.31
  260.1 2.3 fusion.32
  262.7 1.7 fusion.30
  264.4 3.4 fusion.31
  267.8 2.3 fusion.32
  270.4 1.7 fusion.30
  272.1 3.4 fusion.31
  275.5 2.3 fusion.32
  278.1 1.7 fusion.30
  279.8 3.4 fusion.31
  283.2 2.3 fusion.32
  285.7 1.7 fusion.30
  287.5 3.4 fusion.31
  290.9 2.3 fusion.32
  293.4 1.7 fusion.30
  295.1 3.4 fusion.31
  298.5 2.3 fusion.32
  301.0 138.9 %all-to-all-done.2 = bf16[128,128,128]{2,1,0:T(8,128)(2,1)} async-done(((bf16[128,128,128]{2,1,0:T(8,128)(2,1)}), bf16[128,128,128]{2,1,0:T(8,128)(2,1)}, u32[]{:S(2)}, u32[]{:S(2)}) %all-to-all-start.2) | async-done | bytes 4194336 | tf_op jit(solution)/shard_map/all_to_all | solution.py:92
  439.9 4.4 gather_fusion.4
  444.3 11.0 %divide_convert_fusion = bf16[6,1280,128]{2,1,0:T(8,128)(2,1)S(1)} fusion(bf16[6,1280,1280]{1,2,0:T(8,128)(2,1)} %get-tuple-element.49, bf16[6,1280,128]{2,1,0:T(8,128)(2,1)} %bitcast.123, f32[6,1280]{1,0:T(8,128)S(1)} %bitcast.139), kind=kOutput, calls=%fused_computation.22 | convolution fusion | flops 2518548480 | bytes 23623680 | tf_op jit(solution)/shard_map/hqk,hkd->hqd/dot_general | solution.py:137
  455.2 3.1 gather_fusion.5
  458.3 8.9 %all-to-all-start.3 = ((bf16[128,128,128]{2,1,0:T(8,128)(2,1)}), bf16[128,128,128]{2,1,0:T(8,128)(2,1)}, u32[]{:S(2)}, u32[]{:S(2)}) async-start(bf16[128,128,128]{2,1,0:T(8,128)(2,1)} %gather_fusion.5), calls=%async_computation.3 | async-start | bytes 8388608 | tf_op jit(solution)/shard_map/all_to_all | solution.py:141
  467.3 188.1 %all-to-all-done.3 = bf16[128,128,128]{2,1,0:T(8,128)(2,1)} async-done(((bf16[128,128,128]{2,1,0:T(8,128)(2,1)}), bf16[128,128,128]{2,1,0:T(8,128)(2,1)}, u32[]{:S(2)}, u32[]{:S(2)}) %all-to-all-start.3) | async-done | bytes 4194336 | tf_op jit(solution)/shard_map/all_to_all | solution.py:141
  655.4 3.0 gather_fusion.6
  658.6 23.6 %all_to_all.25 = bf16[4,6,2,128,128]{4,3,2,1,0:T(8,128)(2,1)S(1)} all-to-all(bf16[4,6,2,128,128]{4,3,2,1,0:T(8,128)(2,1)S(1)} %copy.71), channel_id=1, replica_groups=mesh['seq'=128,'fsdp'=4] {'fsdp'}, dimensions={0} | all-to-all | bytes 3145728 | tf_op jit(solution)/shard_map/all_to_all | solution.py:147
  683.2 2.6 reshape.392
  (97 shorter events, 14.3 us)
Async XLA Ops:
  0.0 7.4 %copy-start = (s32[24,1024]{1,0:T(8,128)S(1)}, s32[24,1024]{1,0:T(8,128)}, u32[]{:S(2)}) copy-start(s32[24,1024]{1,0:T(8,128)} %param.7) | copy-start | bytes 294916
  2.8 7.2 %copy-start.3 = (bf16[256,3072]{1,0:T(8,128)(2,1)S(1)}, bf16[256,3072]{1,0:T(8,128)(2,1)}, u32[]{:S(2)}) copy-start(bf16[256,3072]{1,0:T(8,128)(2,1)} %param.6) | copy-start | bytes 4718596
  2.8 25.3 %all-to-all-start = ((bf16[4,256,768]{2,1,0:T(8,128)(2,1)}), bf16[4,256,768]{2,1,0:T(8,128)(2,1)S(1)}, u32[]{:S(2)}, u32[]{:S(2)}) async-start(bf16[4,256,768]{2,1,0:T(8,128)(2,1)} %pad_maximum_fusion), calls=%async_computation | async-start | bytes 3145728 | tf_op jit(solution)/shard_map/all_to_all | solution.py:44
  35.7 207.1 %all-to-all-start.1 = ((bf16[128,128,128]{2,1,0:T(8,128)(2,1)}), bf16[128,128,128]{2,1,0:T(8,128)(2,1)}, u32[]{:S(2)}, u32[]{:S(2)}) async-start(bf16[128,128,128]{2,1,0:T(8,128)(2,1)} %gather_fusion), calls=%async_computation.1 | async-start | bytes 8388608 | tf_op jit(solution)/shard_map/all_to_all | solution.py:89
  54.7 3.4 copy-start.2
  58.4 22.7 %collective-permute-start = (bf16[256,768]{1,0:T(8,128)(2,1)S(1)}, bf16[256,768]{1,0:T(8,128)(2,1)S(1)}, u32[]{:S(2)}, u32[]{:S(2)}) collective-permute-start(bf16[256,768]{1,0:T(8,128)(2,1)S(1)} %bitcast.129), channel_id=1, source_target_pairs={{0,1},{1,2},{2,3},{3,0},{4,5},{5,6},{6,7},{7,4},{8,9},{9,10},{10,1... | collective-permute-start | bytes 1179656 | tf_op jit(solution)/shard_map/ppermute | solution.py:58
  61.0 20.0 %collective-permute-start.1 = (bf16[256,768]{1,0:T(8,128)(2,1)S(1)}, bf16[256,768]{1,0:T(8,128)(2,1)S(1)}, u32[]{:S(2)}, u32[]{:S(2)}) collective-permute-start(bf16[256,768]{1,0:T(8,128)(2,1)S(1)} %bitcast.130), channel_id=1, source_target_pairs={{0,2},{1,3},{2,0},{3,1},{4,6},{5,7},{6,4},{7,5},{8,10},{9,11},{10,... | collective-permute-start | bytes 1179656 | tf_op jit(solution)/shard_map/ppermute | solution.py:58
  65.2 18.6 %collective-permute-start.2 = (bf16[256,768]{1,0:T(8,128)(2,1)S(1)}, bf16[256,768]{1,0:T(8,128)(2,1)S(1)}, u32[]{:S(2)}, u32[]{:S(2)}) collective-permute-start(bf16[256,768]{1,0:T(8,128)(2,1)S(1)} %bitcast.131), channel_id=1, source_target_pairs={{0,3},{1,0},{2,1},{3,2},{4,7},{5,4},{6,5},{7,6},{8,11},{9,8},{10,9... | collective-permute-start | bytes 1179656 | tf_op jit(solution)/shard_map/ppermute | solution.py:58
  83.8 0.7 copy-start.4
  242.8 197.1 %all-to-all-start.2 = ((bf16[128,128,128]{2,1,0:T(8,128)(2,1)}), bf16[128,128,128]{2,1,0:T(8,128)(2,1)}, u32[]{:S(2)}, u32[]{:S(2)}) async-start(bf16[128,128,128]{2,1,0:T(8,128)(2,1)} %gather_fusion.2), calls=%async_computation.2 | async-start | bytes 8388608 | tf_op jit(solution)/shard_map/all_to_all | solution.py:92
  458.3 197.1 %all-to-all-start.3 = ((bf16[128,128,128]{2,1,0:T(8,128)(2,1)}), bf16[128,128,128]{2,1,0:T(8,128)(2,1)}, u32[]{:S(2)}, u32[]{:S(2)}) async-start(bf16[128,128,128]{2,1,0:T(8,128)(2,1)} %gather_fusion.5), calls=%async_computation.3 | async-start | bytes 8388608 | tf_op jit(solution)/shard_map/all_to_all | solution.py:141
  682.1 3.7 copy-start.1
